TPU v7x, 512 devices: a whole 4x8x8 slice. The times are simulated.
512 devices in a mesh: req: 64 (over z, x, core), tp: 8 (over y).
Axes of the slice: x: 4, y: 8, z: 8, core: 2. Of those that a mesh axis runs over, the one named last changes fastest.
Arguments:
- q_new: bfloat16 [4096, 5120], P('req', 'tp'), may hold values from -6 to 6
- k_new: bfloat16 [4096, 1024], P('req', 'tp'), may hold values from -15 to 15
- v_new: bfloat16 [4096, 1024], P('req', 'tp'), may hold values from -6 to 6
- k_cache: bfloat16 [1024, 128, 1024], P('req', None, 'tp'), may hold values from -16 to 16
- v_cache: bfloat16 [1024, 128, 1024], P('req', None, 'tp'), may hold values from -6 to 6
- lengths: int32 [32], replicated, may hold values from 1 to 4096, as said below
- page_table: int32 [32, 32], replicated, may hold values from -1 to 1023, as said below
- w_out: bfloat16 [5120, 5120], P('req', 'tp'), may hold values from -0.078125 to 0.078125
Outputs:
- attn_out: bfloat16 [4096, 5120], P('req')
Inputs may be any that keep to these rules, and one draw needn't show every extreme that they name: `lengths`: the last request, 31, has exactly 4096 cached tokens; every request has at least one. `page_table`: request r uses ceil(lengths[r] / 128) logical pages. Its first ceil(ceil(lengths[r] / 128) / 2) logical pages lie among global pages 2r * 16 to (2r + 1) * 16 - 1, the rest among (2r + 1) * 16 to (2r + 2) * 16 - 1; distinct logical pages use distinct global pages; entries past a request's last page are -1.
All inputs are finite; a program needn't handle non-finite values.
Results may differ from a plain program's by a relative error of at most 0.024.
Values may be sent and summed in bfloat16 or wider, within the bound.
No kernel may reach another device: no remote copies, remote signals or barrier semaphores. Data moves between devices by JAX's collectives and lax.ppermute only.
A program may use at most 64 MiB of HBM per device.

v0:
```python
import math
import jax
import jax.numpy as jnp
from jax import lax
from jax.sharding import Mesh
from jax.sharding import PartitionSpec as P

HD = 128
GROUP = 5
ROWS = ("z", "x", "core")
ROPE_BASE = 1000000.0
FLOOR_SCORE = -1e30


def from_partner(value, axis, distance):
    return lax.ppermute(value, axis, [(i, i ^ 1 << distance) for i in range(lax.axis_size(axis))])


def rotate(values, places):
    inverse = 1.0 / ROPE_BASE ** (jnp.arange(0, HD, 2).astype(jnp.float32) / HD)
    angles = places.astype(jnp.float32)[:, None] * inverse[None, :]
    cosine = jnp.concatenate([jnp.cos(angles), jnp.cos(angles)], axis=-1)[:, None, :]
    sine = jnp.concatenate([jnp.sin(angles), jnp.sin(angles)], axis=-1)[:, None, :]
    first_half = values[..., : HD // 2]
    second_half = values[..., HD // 2 :]
    turned = jnp.concatenate([-second_half, first_half], axis=-1)
    return values * cosine + turned * sine


def absorb(state, queries, block_keys, block_values, allowed, scale):
    running_max, running_sum, output = state
    scores = (
        jnp.einsum("qcgd,kcd->cgqk", queries, block_keys, preferred_element_type=jnp.float32)
        * scale
    )
    scores = jnp.where(allowed[None, None], scores, FLOOR_SCORE)
    new_max = jnp.maximum(running_max, jnp.max(scores, axis=-1))
    factor = jnp.exp(running_max - new_max)
    weights = jnp.where(allowed[None, None], jnp.exp(scores - new_max[..., None]), 0.0)
    running_sum = running_sum * factor + jnp.sum(weights, axis=-1)
    mixed = jnp.einsum(
        "cgqk,kcd->qcgd",
        weights.astype(jnp.bfloat16),
        block_values,
        preferred_element_type=jnp.float32,
    )
    output = output * jnp.transpose(factor, (2, 0, 1))[..., None] + mixed
    return (new_max, running_sum, output)


def output_rows(w_out):
    parts = lax.axis_size("tp")
    rows, width = w_out.shape
    share = rows // parts
    pieces = lax.all_to_all(w_out.reshape(parts, share, width), "tp", 0, 0, tiled=True)
    mine = jnp.transpose(pieces, (1, 0, 2))
    near = lax.all_gather(mine, "z", axis=0, tiled=True)
    return (lax.all_gather(near, ("x", "core"), axis=0, tiled=True), share)


def shards(q_new, k_new, v_new, k_cache, v_cache, lengths, page_table, w_out):
    own_rows = q_new.shape[0]
    all_rows = 2 * own_rows
    local_heads = k_new.shape[1] // HD
    pages_local = k_cache.shape[0]
    page_rows = k_cache.shape[1]
    scale = 1.0 / math.sqrt(HD)
    weights_mine, share = output_rows(w_out)
    device_row = (lax.axis_index("z") * lax.axis_size("x") + lax.axis_index("x")) * lax.axis_size(
        "core"
    ) + lax.axis_index("core")
    parity = device_row % 2
    request = device_row // 2
    length = lengths[request]
    own_places = length + parity * own_rows + jnp.arange(own_rows)
    own_queries = rotate(
        q_new.reshape(own_rows, local_heads * GROUP, HD).astype(jnp.float32), own_places
    ).astype(jnp.bfloat16)
    own_keys = rotate(
        k_new.reshape(own_rows, local_heads, HD).astype(jnp.float32), own_places
    ).astype(jnp.bfloat16)
    own_values = v_new.reshape(own_rows, local_heads, HD)
    query_heads = own_queries.shape[1]
    peer_pack = from_partner(
        jnp.concatenate([own_queries, own_keys, own_values], axis=1), "core", 0
    )
    peer_queries = peer_pack[:, :query_heads]
    peer_keys = peer_pack[:, query_heads : query_heads + local_heads]
    peer_values = peer_pack[:, query_heads + local_heads :]

    def ordered(mine, theirs):
        return jnp.where(
            parity == 0,
            jnp.concatenate([mine, theirs], axis=0),
            jnp.concatenate([theirs, mine], axis=0),
        )

    queries = ordered(own_queries, peer_queries).reshape(all_rows, local_heads, GROUP, HD)
    fresh_keys = ordered(own_keys, peer_keys)
    fresh_values = ordered(own_values, peer_values)
    state = (
        jnp.full((local_heads, GROUP, all_rows), FLOOR_SCORE, jnp.float32),
        jnp.zeros((local_heads, GROUP, all_rows), jnp.float32),
        jnp.zeros((all_rows, local_heads, GROUP, HD), jnp.float32),
    )
    token_index = jnp.arange(all_rows)
    causal = (token_index[None, :] <= token_index[:, None]) & (parity == 1)
    state = absorb(state, queries, fresh_keys, fresh_values, causal, scale)
    page_count = (length + page_rows - 1) // page_rows
    even_pages = (page_count + 1) // 2
    first_page = jnp.where(parity == 0, 0, even_pages)
    last_page = jnp.where(parity == 0, even_pages, page_count)
    table_row = page_table[request]
    logical = jnp.arange(table_row.shape[0])
    in_range = (logical >= first_page) & (logical < last_page)
    offset = device_row * pages_local
    slot_ids = jnp.arange(pages_local)
    match = in_range[:, None] & (table_row[:, None] - offset == slot_ids[None, :])
    used = jnp.any(match, axis=0)
    base = jnp.sum(jnp.where(match, logical[:, None], 0), axis=0) * page_rows
    key_places = (base[:, None] + jnp.arange(page_rows)[None, :]).reshape(-1)
    usable = jnp.repeat(used, page_rows) & (key_places < length)
    allowed = jnp.broadcast_to(usable[None, :], (all_rows, pages_local * page_rows))
    pool_keys = k_cache.reshape(pages_local * page_rows, local_heads, HD)
    pool_values = v_cache.reshape(pages_local * page_rows, local_heads, HD)
    half = pool_keys.shape[0] // 2
    for start in (0, half):
        state = absorb(
            state,
            queries,
            pool_keys[start : start + half],
            pool_values[start : start + half],
            allowed[:, start : start + half],
            scale,
        )
    running_max, running_sum, output = state
    peer_start = (1 - parity) * own_rows
    own_start = parity * own_rows
    outgoing = (
        lax.dynamic_slice_in_dim(output, peer_start, own_rows, 0),
        lax.dynamic_slice_in_dim(running_max, peer_start, own_rows, 2),
        lax.dynamic_slice_in_dim(running_sum, peer_start, own_rows, 2),
    )
    outgoing = jnp.concatenate(
        [
            outgoing[0].astype(jnp.bfloat16),
            jnp.transpose(outgoing[1], (2, 0, 1))[..., None].astype(jnp.bfloat16),
            jnp.transpose(outgoing[2], (2, 0, 1))[..., None].astype(jnp.bfloat16),
        ],
        axis=-1,
    )
    incoming = from_partner(outgoing, "core", 0).astype(jnp.float32)
    other_output = incoming[..., :HD]
    other_max = jnp.transpose(incoming[..., HD], (1, 2, 0))
    other_sum = jnp.transpose(incoming[..., HD + 1], (1, 2, 0))
    mine_output = lax.dynamic_slice_in_dim(output, own_start, own_rows, 0)
    mine_max = lax.dynamic_slice_in_dim(running_max, own_start, own_rows, 2)
    mine_sum = lax.dynamic_slice_in_dim(running_sum, own_start, own_rows, 2)
    joint_max = jnp.maximum(mine_max, other_max)
    mine_factor = jnp.exp(mine_max - joint_max)
    other_factor = jnp.exp(other_max - joint_max)
    joint_sum = mine_sum * mine_factor + other_sum * other_factor
    joint_output = (
        mine_output * jnp.transpose(mine_factor, (2, 0, 1))[..., None]
        + other_output * jnp.transpose(other_factor, (2, 0, 1))[..., None]
    )
    attention = (
        (joint_output / jnp.transpose(joint_sum, (2, 0, 1))[..., None])
        .reshape(own_rows, local_heads * GROUP * HD)
        .astype(jnp.bfloat16)
    )
    full_rows = lax.all_gather(attention[:, None], "tp", axis=1, tiled=True)
    projected = lax.dot_general(
        full_rows, weights_mine, (((1, 2), (1, 2)), ((), ())), preferred_element_type=jnp.float32
    )
    depth = lax.axis_size("z")
    projected = projected.reshape(own_rows, -1, depth, share)
    projected = jnp.transpose(projected, (0, 2, 1, 3)).reshape(own_rows, -1, share)
    projected = projected.astype(jnp.bfloat16)
    gathered = lax.all_gather(projected, "tp", axis=2, tiled=True)
    return gathered.reshape(own_rows, -1)


def solution(mesh):
    in_specs = (
        P(ROWS, "tp"),
        P(ROWS, "tp"),
        P(ROWS, "tp"),
        P(ROWS, None, "tp"),
        P(ROWS, None, "tp"),
        P(),
        P(),
        P(ROWS, "tp"),
    )
    out_specs = P(ROWS, None)
    rows, parts = mesh.devices.shape
    cores = 2
    depth = 4 if rows % (4 * cores) == 0 else 1
    split = Mesh(mesh.devices.reshape(depth, rows // (depth * cores), cores, parts), ROWS + ("tp",))
    return jax.shard_map(
        shards, mesh=split, in_specs=in_specs, out_specs=out_specs, check_vma=False
    )
```

profile of v0, /device:TPU:6, one launch (start us, length us, event | category | flops | bytes accessed | tf_op | source)
XLA Modules:
  0.0 135.1 jit_solution(9151260461402743674)
XLA Ops:
  6.5 0.0 copy-start.3
  6.5 0.0 copy-start.6
  6.5 0.0 copy-start.5
  6.5 0.0 all-gather.2.cloned.1.call-start
  6.6 1.0 reshape.452
  7.6 16.7 %all_to_all.5 = bf16[8,10,640]{2,1,0:T(8,128)(2,1)S(1)} all-to-all(bf16[8,10,640]{2,1,0:T(8,128)(2,1)S(1)} %reshape.452), channel_id=1, replica_groups=mesh['z'=4,'x'=8,'core'=2,'tp'=8] {'tp'}, dimensions={0} | all-to-all | bytes 204800 | tf_op jit(solution)/shard_map/all_to_all | solution.py:55
  24.2 0.0 copy-start.1
  24.3 21.0 %all_gather.13 = bf16[40,8,640]{2,1,0:T(8,128)(2,1)S(1)} all-gather(bf16[10,8,640]{2,1,0:T(8,128)(2,1)S(1)} %copy.92), channel_id=1, replica_groups=mesh['z'=4,'x'=8,'core'=2,'tp'=8] {'z'}, dimensions={0}, use_global_device_ids=true | all-gather | bytes 512000 | tf_op jit(solution)/shard_map/all_gather | solution.py:57
  45.3 0.8 copy.93
  46.0 0.0 copy-start.2
  46.1 0.0 all-gather.2.cloned.1.call-update
  46.1 0.0 copy-done.3
  46.1 0.1 reshape.454
  46.2 0.0 copy-done.6
  46.2 0.6 dynamic_slice.24
  47.5 0.0 copy-done.4
  47.5 0.2 multiply_cosine_fusion
  47.7 0.1 fusion.54
  47.8 0.1 pad_maximum_fusion.2
  48.0 0.0 copy-done.5
  48.0 0.1 slice_negate_fusion
  48.1 0.1 fusion.41
  48.3 0.1 pad_maximum_fusion.1
  48.4 1.9 %collective-permute-start = (bf16[64,7,128]{2,1,0:T(8,128)(2,1)S(1)}, bf16[64,7,128]{2,1,0:T(8,128)(2,1)S(1)}, u32[]{:S(2)}, u32[]{:S(2)}) collective-permute-start(bf16[64,7,128]{2,1,0:T(8,128)(2,1)S(1)} %pad_maximum_fusion.1), channel_id=1, source_target_pairs={{0,8},{8,0},{1,9},{9,1},{2,10},{10,2},{3,11},{11,3},{4,12},{12,4},... | collective-permute-start | bytes 344072 | tf_op jit(solution)/shard_map/ppermute | solution.py:16
  51.1 0.7 fusion.97
  51.8 0.1 fusion.77
  51.9 0.1 select_reduce_fusion
  52.0 0.7 fusion.79
  52.7 0.0 copy-done.1
  52.8 0.0 copy-done.2
  52.8 0.8 fusion.110
  53.6 0.0 collective-permute-done
  53.6 0.1 fusion.112
  53.7 0.1 maximum_select_fusion
  53.9 0.2 fusion.113
  54.1 0.6 fusion.2
  54.7 0.0 copy-start
  54.7 0.6 fusion.3
  55.4 0.1 fusion.38
  55.4 1.5 %fusion.4 = (f32[5,128]{1,0:T(8,128)S(1)}, f32[5,128]{1,0:T(8,128)S(1)}) fusion(f32[128,5,1024]{2,0,1:T(8,128)S(1)} %get-tuple-element.38, f32[5,128]{1,0:T(8,128)S(1)} %get-tuple-element.10, pred[1024]{0:T(1024)(128)(4,1)S(1)} %get-tuple-element.8, f32[5,128]{1,0:T(8,128)S(1)} %get-tuple-element.9, f32[128,5,1024]{2,0,1:T(8,128)S(1)} %get-tuple-element.36, ...), kind=kLoop, calls=%fused_computation.8 | loop fusion | flops 6552320 | bytes 5255168 | tf_op jit(solution)/shard_map/reduce_sum | solution.py:40
  56.9 0.0 copy-done
  57.0 0.1 fusion.90
  57.0 0.1 copy.87
  57.2 0.1 fusion.91
  57.3 0.1 copy.88
  57.4 0.3 fusion.35
  57.7 2.5 %fusion.31 = f32[128,1,5,128]{3,0,2,1:T(8,128)S(1)} fusion(f32[128,1,5,128]{3,0,2,1:T(8,128)S(1)} %fusion.35, bf16[1024,128,1]{1,0,2:T(8,128)(2,1)} %bitcast.311, f32[128,5,1024]{2,0,1:T(8,128)} %copy-done, f32[5,128]{1,0:T(8,128)S(1)} %get-tuple-element.10, pred[1024]{0:T(1024)(128)(4,1)S(1)} %get-tuple-element.8, f32[128,5]{0,1:T(8,128)S(1)} %get-tuple-element.24), kind=kOutput, calls=%fused_computation.27 | convolution fusion | flops 171212800 | bytes 3545088 | tf_op jit(solution)/shard_map/cgqk,kcd->qcgd/dot_general | solution.py:41
  60.2 0.7 fusion.28
  61.0 0.1 pad_maximum_fusion
  61.1 2.4 %collective-permute-start.1 = (bf16[64,1,5,130]{3,0,2,1:T(8,128)(2,1)S(1)}, bf16[64,1,5,130]{3,0,2,1:T(8,128)(2,1)S(1)}, u32[]{:S(2)}, u32[]{:S(2)}) collective-permute-start(bf16[64,1,5,130]{3,0,2,1:T(8,128)(2,1)S(1)} %pad_maximum_fusion), channel_id=1, source_target_pairs={{0,8},{8,0},{1,9},{9,1},{2,10},{10,2},{3,11},{11,3},{4,12},{12,4},... | collective-permute-start | bytes 249608 | tf_op jit(solution)/shard_map/ppermute | solution.py:16
  63.5 1.0 collective-permute-done.1
  64.5 0.2 slice_reduce_fusion.1
  64.8 0.1 fusion.95
  64.8 0.2 copy_bitcast_fusion
  65.1 25.7 %all_gather.12 = bf16[64,8,640]{2,0,1:T(8,128)(2,1)S(1)} all-gather(bf16[64,1,640]{2,0,1:T(8,128)(2,1)S(1)} %copy_bitcast_fusion), channel_id=1, replica_groups=mesh['z'=4,'x'=8,'core'=2,'tp'=8] {'tp'}, dimensions={1}, use_global_device_ids=true | all-gather | bytes 737280 | tf_op jit(solution)/shard_map/all_gather | solution.py:172
  90.7 0.0 all-gather.2.cloned.1.call-done
  90.7 4.9 %fusion.37 = bf16[64,640]{1,0:T(8,128)(2,1)S(1)} fusion(bf16[64,8,640]{2,0,1:T(8,128)(2,1)S(1)} %all_gather.12, bf16[640,8,640]{2,0,1:T(8,128)(2,1)} %all-gather.2.cloned.1.call-done), kind=kOutput, calls=%fused_computation.32 | convolution fusion | flops 419471360 | bytes 7290880 | tf_op jit(solution)/shard_map/dot_general | solution.py:173
  95.7 0.2 copy.94
  95.8 0.1 convert_element_type.134
  95.9 0.1 copy.95
  96.0 0.1 copy.96
  96.2 27.6 %all_gather.15 = bf16[64,64,80]{1,0,2:T(8,128)(2,1)S(1)} all-gather(bf16[64,64,10]{1,0,2:T(8,128)(2,1)S(1)} %copy.96), channel_id=1, replica_groups=mesh['z'=4,'x'=8,'core'=2,'tp'=8] {'tp'}, dimensions={2}, use_global_device_ids=true | all-gather | bytes 737280 | tf_op jit(solution)/shard_map/all_gather | solution.py:180
  123.8 1.5 %copy.97 = bf16[64,64,80]{2,1,0:T(8,128)(2,1)S(1)} copy(bf16[64,64,80]{1,0,2:T(8,128)(2,1)S(1)} %all_gather.15) | data formatting | bytes 1310720 | tf_op jit(solution)/shard_map/all_gather | solution.py:180
  125.3 2.9 %reshape.453 = bf16[64,5120]{1,0:T(8,128)(2,1)} reshape(bf16[64,64,80]{2,1,0:T(8,128)(2,1)S(1)} %copy.97) | data formatting | bytes 1310720 | tf_op jit(solution)/shard_map/reshape | solution.py:181
  (19 shorter events, 0.3 us)
Async XLA Ops:
  6.5 39.6 %copy-start.3 = (bf16[64,640]{1,0:T(8,128)(2,1)S(1)}, bf16[64,640]{1,0:T(8,128)(2,1)}, u32[]{:S(2)}) copy-start(bf16[64,640]{1,0:T(8,128)(2,1)} %param.8) | copy-start | bytes 245764
  6.5 39.7 %copy-start.6 = (s32[32]{0:T(128)S(1)}, s32[32]{0:T(128)}, u32[]{:S(2)}) copy-start(s32[32]{0:T(128)} %param.13) | copy-start | bytes 388
  6.5 41.0 %copy-start.4 = (bf16[64,128]{1,0:T(8,128)(2,1)S(1)}, bf16[64,128]{1,0:T(8,128)(2,1)}, u32[]{:S(2)}) copy-start(bf16[64,128]{1,0:T(8,128)(2,1)} %param.9) | copy-start | bytes 49156
  6.5 41.4 %copy-start.5 = (bf16[64,128]{1,0:T(8,128)(2,1)S(1)}, bf16[64,128]{1,0:T(8,128)(2,1)}, u32[]{:S(2)}) copy-start(bf16[64,128]{1,0:T(8,128)(2,1)} %param.10) | copy-start | bytes 49156
  6.5 84.2 %all-gather.2.cloned.1.call-start = ((), (), s32[]{:S(2)}) async-start(), calls=%async_computation.1 | async-start | bytes 6963200 | tf_op jit(solution)/shard_map/all_gather | solution.py:58
  24.2 28.5 %copy-start.1 = (bf16[16,128,128]{2,1,0:T(8,128)(2,1)S(1)}, bf16[16,128,128]{2,1,0:T(8,128)(2,1)}, u32[]{:S(2)}) copy-start(bf16[16,128,128]{2,1,0:T(8,128)(2,1)} %param.11) | copy-start | bytes 1572868
  46.0 6.7 %copy-start.2 = (bf16[16,128,128]{2,1,0:T(8,128)(2,1)S(1)}, bf16[16,128,128]{2,1,0:T(8,128)(2,1)}, u32[]{:S(2)}) copy-start(bf16[16,128,128]{2,1,0:T(8,128)(2,1)} %param.12) | copy-start | bytes 1572868
  48.4 5.2 %collective-permute-start = (bf16[64,7,128]{2,1,0:T(8,128)(2,1)S(1)}, bf16[64,7,128]{2,1,0:T(8,128)(2,1)S(1)}, u32[]{:S(2)}, u32[]{:S(2)}) collective-permute-start(bf16[64,7,128]{2,1,0:T(8,128)(2,1)S(1)} %pad_maximum_fusion.1), channel_id=1, source_target_pairs={{0,8},{8,0},{1,9},{9,1},{2,10},{10,2},{3,11},{11,3},{4,12},{12,4},... | collective-permute-start | bytes 344072 | tf_op jit(solution)/shard_map/ppermute | solution.py:16
  54.7 2.2 %copy-start = (f32[128,5,1024]{2,0,1:T(8,128)}, f32[128,5,1024]{2,0,1:T(8,128)S(1)}, u32[]{:S(2)}) copy-start(f32[128,5,1024]{2,0,1:T(8,128)S(1)} %get-tuple-element.38) | copy-start | bytes 7864324
  61.1 3.4 %collective-permute-start.1 = (bf16[64,1,5,130]{3,0,2,1:T(8,128)(2,1)S(1)}, bf16[64,1,5,130]{3,0,2,1:T(8,128)(2,1)S(1)}, u32[]{:S(2)}, u32[]{:S(2)}) collective-permute-start(bf16[64,1,5,130]{3,0,2,1:T(8,128)(2,1)S(1)} %pad_maximum_fusion), channel_id=1, source_target_pairs={{0,8},{8,0},{1,9},{9,1},{2,10},{10,2},{3,11},{11,3},{4,12},{12,4},... | collective-permute-start | bytes 249608 | tf_op jit(solution)/shard_map/ppermute | solution.py:16
Sparse Core Ops, SparseCore 0:
  46.2 43.5 all-gather.1
where the time goes:
time: 135 us
  blocking collectives  90.9 us (67%)
  between operations  15.1 us (11%)
  matrix products  9.93 us (7%)
  local copies, waits for them, and re-layouts  9.09 us (7%)
  other arithmetic  4.56 us (3%)
  starting transfers between devices  4.38 us (3%)
    all_gather x1, blocking collectives, shards(): gathered = lax.all_gather(projected, 'tp', axis=2, tiled=True)  27.6 us
    all_gather x1, blocking collectives, shards(): full_rows = lax.all_gather(attention[:, None], 'tp', axis=1, tiled=True)  25.7 us
    all_gather x1, blocking collectives, output_rows(): near = lax.all_gather(mine, 'z', axis=0, tiled=True)  21 us
    all_to_all x1, blocking collectives, output_rows(): lax.all_to_all(w_out.reshape(parts, share, width), 'tp', 0, 0, tiled=True)  16.7 us
    dot_general x1, matrix products, shards(): lax.dot_general(full_rows, weights_mine, (((1, 2), (1, 2)), ((), ())), pr...  4.94 us
    ppermute x2, starting transfers between devices, from_partner(): lax.ppermute(value, axis, [(i, i ^ 1 << distance) for i in range(lax.axis...  4.35 us
    dot_general x3, matrix products, absorb(): jnp.einsum('cgqk,kcd->qcgd', weights.astype(jnp.bfloat16), block_values,...  3.52 us
    reshape x1, local copies, waits for them, and re-layouts, shards(): return gathered.reshape(own_rows, -1)  2.92 us
  transfers between devices with their start and end apart: 3, of which 1 were waited for; matrix products, arithmetic and copies ran while one was open for 9% of the time, Pallas kernels for 0%

commit v1 on v0

--- a/solution.py
+++ b/solution.py
@@ -10,6 +10,18 @@
 ROWS = ("z", "x", "core")
 ROPE_BASE = 1000000.0
 FLOOR_SCORE = -1e30
+
+
+def set_open(xx, row_axis):
+    dev_n = jax.lax.axis_size(row_axis)
+    table = list(map(lambda h: (h, (h + 1) % dev_n), range(dev_n)))
+    piece_now = [None] * dev_n
+    piece_now[dev_n - 1] = xx
+    for num in range(dev_n - 2, -1, -1):
+        piece_now[num] = jax.lax.ppermute(piece_now[num + 1], row_axis, perm=table)
+    return jnp.roll(
+        jnp.concatenate(piece_now, 2), (jax.lax.axis_index(row_axis) + 1) * xx.shape[2], 2
+    )
 
 
 def from_partner(value, axis, distance):
@@ -177,7 +189,7 @@
     projected = projected.reshape(own_rows, -1, depth, share)
     projected = jnp.transpose(projected, (0, 2, 1, 3)).reshape(own_rows, -1, share)
     projected = projected.astype(jnp.bfloat16)
-    gathered = lax.all_gather(projected, "tp", axis=2, tiled=True)
+    gathered = set_open(projected, "tp")
     return gathered.reshape(own_rows, -1)
 
 

time: 135 us -> 171 us (1.27)
  waiting for transfers between devices: 1.02 us -> 47.7 us
  blocking collectives: 90.9 us -> 63.3 us
  starting transfers between devices: 4.38 us -> 18.8 us
    ppermute x0 -> x7, waiting for transfers between devices: none -> 46.6 us  [set_open(): piece_now[num] = jax.lax.ppermute(piece_now[num + 1], row_axis, perm=table)]
    all_gather x1 -> x0, blocking collectives: 27.6 us -> none  [shards(): gathered = lax.all_gather(projected, 'tp', axis=2, tiled=True)]
    ppermute x0 -> x7, starting transfers between devices: none -> 14.4 us  [set_open(): piece_now[num] = jax.lax.ppermute(piece_now[num + 1], row_axis, perm=table)]
    dynamic_slice x0 -> x2, local copies, waits for them, and re-layouts: none -> 2.53 us  [set_open(): jnp.roll(jnp.concatenate(piece_now, 2), (jax.lax.axis_index(row_axis) + 1...]
  transfers between devices with their start and end apart: 3 -> 10, of which waited for: 1 -> 8; matrix products, arithmetic and copies ran while one was open for 9% -> 7% of each run, Pallas kernels for 0% -> 0%
where the time goes in v1:
time: 171 us; the launch traced here: 170 us
  blocking collectives  63.3 us (37%)
  waiting for transfers between devices  47.7 us (28%)
  starting transfers between devices  18.8 us (11%)
  between operations  15.3 us (9%)
  local copies, waits for them, and re-layouts  10.4 us (6%)
  matrix products  9.93 us (6%)
  other arithmetic  4.56 us (3%)
    ppermute x7, waiting for transfers between devices, set_open(): piece_now[num] = jax.lax.ppermute(piece_now[num + 1], row_axis, perm=table)  46.6 us
    all_gather x1, blocking collectives, shards(): full_rows = lax.all_gather(attention[:, None], 'tp', axis=1, tiled=True)  25.7 us
    all_gather x1, blocking collectives, output_rows(): near = lax.all_gather(mine, 'z', axis=0, tiled=True)  21 us
    all_to_all x1, blocking collectives, output_rows(): lax.all_to_all(w_out.reshape(parts, share, width), 'tp', 0, 0, tiled=True)  16.7 us
    ppermute x7, starting transfers between devices, set_open(): piece_now[num] = jax.lax.ppermute(piece_now[num + 1], row_axis, perm=table)  14.4 us
    dot_general x1, matrix products, shards(): lax.dot_general(full_rows, weights_mine, (((1, 2), (1, 2)), ((), ())), pr...  4.94 us
    ppermute x2, starting transfers between devices, from_partner(): lax.ppermute(value, axis, [(i, i ^ 1 << distance) for i in range(lax.axis...  4.35 us
    dot_general x3, matrix products, absorb(): jnp.einsum('cgqk,kcd->qcgd', weights.astype(jnp.bfloat16), block_values,...  3.52 us
  transfers between devices with their start and end apart: 10, of which 8 were waited for; matrix products, arithmetic and copies ran while one was open for 7% of the time, Pallas kernels for 0%

profile of v1, /device:TPU:6, one launch (start us, length us, event | category | flops | bytes accessed | tf_op | source)
XLA Modules:
  0.0 170.0 jit_solution(14512585018866489349)
XLA Ops:
  6.5 0.0 all-gather.2.cloned.1.call-start
  6.6 1.0 reshape.452
  7.6 16.7 %all_to_all.5 = bf16[8,10,640]{2,1,0:T(8,128)(2,1)S(1)} all-to-all(bf16[8,10,640]{2,1,0:T(8,128)(2,1)S(1)} %reshape.452), channel_id=1, replica_groups=mesh['z'=4,'x'=8,'core'=2,'tp'=8] {'tp'}, dimensions={0} | all-to-all | bytes 204800 | tf_op jit(solution)/shard_map/all_to_all | solution.py:67
  24.2 0.0 copy-start.1
  24.3 21.0 %all_gather.10 = bf16[40,8,640]{2,1,0:T(8,128)(2,1)S(1)} all-gather(bf16[10,8,640]{2,1,0:T(8,128)(2,1)S(1)} %copy.91), channel_id=1, replica_groups=mesh['z'=4,'x'=8,'core'=2,'tp'=8] {'z'}, dimensions={0}, use_global_device_ids=true | all-gather | bytes 512000 | tf_op jit(solution)/shard_map/all_gather | solution.py:69
  45.3 0.8 copy.92
  46.1 0.0 all-gather.2.cloned.1.call-update
  46.1 0.1 reshape.454
  46.2 0.6 dynamic_slice.28
  47.5 0.2 multiply_cosine_fusion
  47.7 0.1 fusion.54
  47.8 0.1 pad_maximum_fusion.2
  48.0 0.1 slice_negate_fusion
  48.2 0.1 fusion.41
  48.3 0.1 pad_maximum_fusion.1
  48.4 1.9 %collective-permute-start = (bf16[64,7,128]{2,1,0:T(8,128)(2,1)S(1)}, bf16[64,7,128]{2,1,0:T(8,128)(2,1)S(1)}, u32[]{:S(2)}, u32[]{:S(2)}) collective-permute-start(bf16[64,7,128]{2,1,0:T(8,128)(2,1)S(1)} %pad_maximum_fusion.1), channel_id=1, source_target_pairs={{0,8},{8,0},{1,9},{9,1},{2,10},{10,2},{3,11},{11,3},{4,12},{12,4},... | collective-permute-start | bytes 344072 | tf_op jit(solution)/shard_map/ppermute | solution.py:28
  51.1 0.7 fusion.97
  51.8 0.1 fusion.77
  51.9 0.1 select_reduce_fusion
  52.0 0.7 fusion.79
  52.8 0.8 fusion.110
  53.6 0.0 collective-permute-done
  53.6 0.1 fusion.112
  53.7 0.1 maximum_select_fusion
  53.9 0.2 fusion.113
  54.1 0.6 fusion.2
  54.7 0.6 fusion.3
  55.4 0.1 fusion.38
  55.4 1.5 fusion.4
  57.0 0.1 fusion.90
  57.0 0.1 copy.86
  57.2 0.1 fusion.91
  57.3 0.1 copy.87
  57.4 0.3 fusion.35
  57.7 2.5 %fusion.31 = f32[128,1,5,128]{3,0,2,1:T(8,128)S(1)} fusion(f32[128,1,5,128]{3,0,2,1:T(8,128)S(1)} %fusion.35, bf16[1024,128,1]{1,0,2:T(8,128)(2,1)} %bitcast.313, f32[128,5,1024]{2,0,1:T(8,128)} %copy-done, f32[5,128]{1,0:T(8,128)S(1)} %get-tuple-element.10, pred[1024]{0:T(1024)(128)(4,1)S(1)} %get-tuple-element.8, f32[128,5]{0,1:T(8,128)S(1)} %get-tuple-element.24), kind=kOutput, calls=%fused_computation.27 | convolution fusion | flops 171212800 | bytes 3545088 | tf_op jit(solution)/shard_map/cgqk,kcd->qcgd/dot_general | solution.py:53
  60.2 0.7 fusion.28
  61.0 0.1 pad_maximum_fusion
  61.1 2.4 %collective-permute-start.1 = (bf16[64,1,5,130]{3,0,2,1:T(8,128)(2,1)S(1)}, bf16[64,1,5,130]{3,0,2,1:T(8,128)(2,1)S(1)}, u32[]{:S(2)}, u32[]{:S(2)}) collective-permute-start(bf16[64,1,5,130]{3,0,2,1:T(8,128)(2,1)S(1)} %pad_maximum_fusion), channel_id=1, source_target_pairs={{0,8},{8,0},{1,9},{9,1},{2,10},{10,2},{3,11},{11,3},{4,12},{12,4},... | collective-permute-start | bytes 249608 | tf_op jit(solution)/shard_map/ppermute | solution.py:28
  63.5 1.0 collective-permute-done.1
  64.5 0.2 slice_reduce_fusion.1
  64.8 0.1 fusion.95
  64.8 0.2 copy_bitcast_fusion
  65.1 25.7 %all_gather.9 = bf16[64,8,640]{2,0,1:T(8,128)(2,1)S(1)} all-gather(bf16[64,1,640]{2,0,1:T(8,128)(2,1)S(1)} %copy_bitcast_fusion), channel_id=1, replica_groups=mesh['z'=4,'x'=8,'core'=2,'tp'=8] {'tp'}, dimensions={1}, use_global_device_ids=true | all-gather | bytes 737280 | tf_op jit(solution)/shard_map/all_gather | solution.py:184
  90.7 4.9 %fusion.37 = bf16[64,640]{1,0:T(8,128)(2,1)S(1)} fusion(bf16[64,8,640]{2,0,1:T(8,128)(2,1)S(1)} %all_gather.9, bf16[640,8,640]{2,0,1:T(8,128)(2,1)} %all-gather.2.cloned.1.call-done), kind=kOutput, calls=%fused_computation.32 | convolution fusion | flops 419471360 | bytes 7290880 | tf_op jit(solution)/shard_map/dot_general | solution.py:185
  95.7 0.2 copy.93
  95.8 0.1 convert_element_type.134
  95.9 0.1 copy.94
  96.0 2.5 %collective-permute-start.2 = (bf16[64,64,10]{0,1,2:T(8,128)(2,1)S(1)}, bf16[64,64,10]{0,1,2:T(8,128)(2,1)S(1)}, u32[]{:S(2)}, u32[]{:S(2)}) collective-permute-start(bf16[64,64,10]{0,1,2:T(8,128)(2,1)S(1)} %bitcast.304), channel_id=1, source_target_pairs={{0,1},{1,2},{2,3},{3,4},{4,5},{5,6},{6,7},{7,0},{8,9},{9,10},{10,1... | collective-permute-start | bytes 245768 | tf_op jit(solution)/shard_map/ppermute | solution.py:21
  98.5 6.0 %collective-permute-done.2 = bf16[64,64,10]{0,1,2:T(8,128)(2,1)S(1)} collective-permute-done((bf16[64,64,10]{0,1,2:T(8,128)(2,1)S(1)}, bf16[64,64,10]{0,1,2:T(8,128)(2,1)S(1)}, u32[]{:S(2)}, u32[]{:S(2)}) %collective-permute-start.2) | collective-permute-done | bytes 81952 | tf_op jit(solution)/shard_map/ppermute | solution.py:21
  104.6 2.2 %collective-permute-start.3 = (bf16[64,64,10]{0,1,2:T(8,128)(2,1)S(1)}, bf16[64,64,10]{0,1,2:T(8,128)(2,1)S(1)}, u32[]{:S(2)}, u32[]{:S(2)}) collective-permute-start(bf16[64,64,10]{0,1,2:T(8,128)(2,1)S(1)} %collective-permute-done.2), channel_id=1, source_target_pairs={{0,1},{1,2},{2,3},{3,4},{4,5},{5,6},{6,7},{7,0},{8,9},{9,10},{10,1... | collective-permute-start | bytes 245768 | tf_op jit(solution)/shard_map/ppermute | solution.py:21
  106.8 6.2 %collective-permute-done.3 = bf16[64,64,10]{0,1,2:T(8,128)(2,1)S(1)} collective-permute-done((bf16[64,64,10]{0,1,2:T(8,128)(2,1)S(1)}, bf16[64,64,10]{0,1,2:T(8,128)(2,1)S(1)}, u32[]{:S(2)}, u32[]{:S(2)}) %collective-permute-start.3) | collective-permute-done | bytes 81952 | tf_op jit(solution)/shard_map/ppermute | solution.py:21
  113.0 1.9 %collective-permute-start.4 = (bf16[64,64,10]{0,1,2:T(8,128)(2,1)S(1)}, bf16[64,64,10]{0,1,2:T(8,128)(2,1)S(1)}, u32[]{:S(2)}, u32[]{:S(2)}) collective-permute-start(bf16[64,64,10]{0,1,2:T(8,128)(2,1)S(1)} %collective-permute-done.3), channel_id=1, source_target_pairs={{0,1},{1,2},{2,3},{3,4},{4,5},{5,6},{6,7},{7,0},{8,9},{9,10},{10,1... | collective-permute-start | bytes 245768 | tf_op jit(solution)/shard_map/ppermute | solution.py:21
  114.9 6.5 %collective-permute-done.4 = bf16[64,64,10]{0,1,2:T(8,128)(2,1)S(1)} collective-permute-done((bf16[64,64,10]{0,1,2:T(8,128)(2,1)S(1)}, bf16[64,64,10]{0,1,2:T(8,128)(2,1)S(1)}, u32[]{:S(2)}, u32[]{:S(2)}) %collective-permute-start.4) | collective-permute-done | bytes 81952 | tf_op jit(solution)/shard_map/ppermute | solution.py:21
  121.4 1.9 %collective-permute-start.5 = (bf16[64,64,10]{0,1,2:T(8,128)(2,1)S(1)}, bf16[64,64,10]{0,1,2:T(8,128)(2,1)S(1)}, u32[]{:S(2)}, u32[]{:S(2)}) collective-permute-start(bf16[64,64,10]{0,1,2:T(8,128)(2,1)S(1)} %collective-permute-done.4), channel_id=1, source_target_pairs={{0,1},{1,2},{2,3},{3,4},{4,5},{5,6},{6,7},{7,0},{8,9},{9,10},{10,1... | collective-permute-start | bytes 245768 | tf_op jit(solution)/shard_map/ppermute | solution.py:21
  123.3 6.5 %collective-permute-done.5 = bf16[64,64,10]{0,1,2:T(8,128)(2,1)S(1)} collective-permute-done((bf16[64,64,10]{0,1,2:T(8,128)(2,1)S(1)}, bf16[64,64,10]{0,1,2:T(8,128)(2,1)S(1)}, u32[]{:S(2)}, u32[]{:S(2)}) %collective-permute-start.5) | collective-permute-done | bytes 81952 | tf_op jit(solution)/shard_map/ppermute | solution.py:21
  129.8 1.9 %collective-permute-start.6 = (bf16[64,64,10]{0,1,2:T(8,128)(2,1)S(1)}, bf16[64,64,10]{0,1,2:T(8,128)(2,1)S(1)}, u32[]{:S(2)}, u32[]{:S(2)}) collective-permute-start(bf16[64,64,10]{0,1,2:T(8,128)(2,1)S(1)} %collective-permute-done.5), channel_id=1, source_target_pairs={{0,1},{1,2},{2,3},{3,4},{4,5},{5,6},{6,7},{7,0},{8,9},{9,10},{10,1... | collective-permute-start | bytes 245768 | tf_op jit(solution)/shard_map/ppermute | solution.py:21
  131.7 7.0 %collective-permute-done.6 = bf16[64,64,10]{0,1,2:T(8,128)(2,1)S(1)} collective-permute-done((bf16[64,64,10]{0,1,2:T(8,128)(2,1)S(1)}, bf16[64,64,10]{0,1,2:T(8,128)(2,1)S(1)}, u32[]{:S(2)}, u32[]{:S(2)}) %collective-permute-start.6) | collective-permute-done | bytes 81952 | tf_op jit(solution)/shard_map/ppermute | solution.py:21
  138.7 1.9 %collective-permute-start.7 = (bf16[64,64,10]{0,1,2:T(8,128)(2,1)S(1)}, bf16[64,64,10]{0,1,2:T(8,128)(2,1)S(1)}, u32[]{:S(2)}, u32[]{:S(2)}) collective-permute-start(bf16[64,64,10]{0,1,2:T(8,128)(2,1)S(1)} %collective-permute-done.6), channel_id=1, source_target_pairs={{0,1},{1,2},{2,3},{3,4},{4,5},{5,6},{6,7},{7,0},{8,9},{9,10},{10,1... | collective-permute-start | bytes 245768 | tf_op jit(solution)/shard_map/ppermute | solution.py:21
  140.6 8.1 %collective-permute-done.7 = bf16[64,64,10]{0,1,2:T(8,128)(2,1)S(1)} collective-permute-done((bf16[64,64,10]{0,1,2:T(8,128)(2,1)S(1)}, bf16[64,64,10]{0,1,2:T(8,128)(2,1)S(1)}, u32[]{:S(2)}, u32[]{:S(2)}) %collective-permute-start.7) | collective-permute-done | bytes 81952 | tf_op jit(solution)/shard_map/ppermute | solution.py:21
  148.7 2.1 %collective-permute-start.8 = (bf16[64,64,10]{0,1,2:T(8,128)(2,1)S(1)}, bf16[64,64,10]{0,1,2:T(8,128)(2,1)S(1)}, u32[]{:S(2)}, u32[]{:S(2)}) collective-permute-start(bf16[64,64,10]{0,1,2:T(8,128)(2,1)S(1)} %collective-permute-done.7), channel_id=1, source_target_pairs={{0,1},{1,2},{2,3},{3,4},{4,5},{5,6},{6,7},{7,0},{8,9},{9,10},{10,1... | collective-permute-start | bytes 245768 | tf_op jit(solution)/shard_map/ppermute | solution.py:21
  150.9 6.3 %collective-permute-done.8 = bf16[64,64,10]{0,1,2:T(8,128)(2,1)S(1)} collective-permute-done((bf16[64,64,10]{0,1,2:T(8,128)(2,1)S(1)}, bf16[64,64,10]{0,1,2:T(8,128)(2,1)S(1)}, u32[]{:S(2)}, u32[]{:S(2)}) %collective-permute-start.8) | collective-permute-done | bytes 81952 | tf_op jit(solution)/shard_map/ppermute | solution.py:21
  157.6 0.1 constant_dynamic-slice_fusion
  157.7 2.4 %copy.95 = bf16[64,64,80]{2,1,0:T(8,128)(2,1)S(1)} copy(bf16[64,64,80]{0,1,2:T(8,128)(2,1)S(1)} %constant_dynamic-slice_fusion) | data formatting | bytes 1310720 | tf_op jit(solution)/shard_map/jit(_roll_dynamic)/dynamic_slice | solution.py:22
  160.2 2.9 %reshape.453 = bf16[64,5120]{1,0:T(8,128)(2,1)} reshape(bf16[64,64,80]{2,1,0:T(8,128)(2,1)S(1)} %copy.95) | data formatting | bytes 1310720 | tf_op jit(solution)/shard_map/reshape | solution.py:193
  (48 shorter events, 0.7 us)
Async XLA Ops:
  6.5 39.6 %copy-start.3 = (bf16[64,640]{1,0:T(8,128)(2,1)S(1)}, bf16[64,640]{1,0:T(8,128)(2,1)}, u32[]{:S(2)}) copy-start(bf16[64,640]{1,0:T(8,128)(2,1)} %param.8) | copy-start | bytes 245764
  6.5 39.7 %copy-start.6 = (s32[32]{0:T(128)S(1)}, s32[32]{0:T(128)}, u32[]{:S(2)}) copy-start(s32[32]{0:T(128)} %param.13) | copy-start | bytes 388
  6.5 41.0 %copy-start.4 = (bf16[64,128]{1,0:T(8,128)(2,1)S(1)}, bf16[64,128]{1,0:T(8,128)(2,1)}, u32[]{:S(2)}) copy-start(bf16[64,128]{1,0:T(8,128)(2,1)} %param.9) | copy-start | bytes 49156
  6.5 41.4 %copy-start.5 = (bf16[64,128]{1,0:T(8,128)(2,1)S(1)}, bf16[64,128]{1,0:T(8,128)(2,1)}, u32[]{:S(2)}) copy-start(bf16[64,128]{1,0:T(8,128)(2,1)} %param.10) | copy-start | bytes 49156
  6.5 84.2 %all-gather.2.cloned.1.call-start = ((), (), s32[]{:S(2)}) async-start(), calls=%async_computation.1 | async-start | bytes 6963200 | tf_op jit(solution)/shard_map/all_gather | solution.py:70
  24.2 28.5 %copy-start.1 = (bf16[16,128,128]{2,1,0:T(8,128)(2,1)S(1)}, bf16[16,128,128]{2,1,0:T(8,128)(2,1)}, u32[]{:S(2)}) copy-start(bf16[16,128,128]{2,1,0:T(8,128)(2,1)} %param.11) | copy-start | bytes 1572868
  46.0 6.7 %copy-start.2 = (bf16[16,128,128]{2,1,0:T(8,128)(2,1)S(1)}, bf16[16,128,128]{2,1,0:T(8,128)(2,1)}, u32[]{:S(2)}) copy-start(bf16[16,128,128]{2,1,0:T(8,128)(2,1)} %param.12) | copy-start | bytes 1572868
  48.4 5.2 %collective-permute-start = (bf16[64,7,128]{2,1,0:T(8,128)(2,1)S(1)}, bf16[64,7,128]{2,1,0:T(8,128)(2,1)S(1)}, u32[]{:S(2)}, u32[]{:S(2)}) collective-permute-start(bf16[64,7,128]{2,1,0:T(8,128)(2,1)S(1)} %pad_maximum_fusion.1), channel_id=1, source_target_pairs={{0,8},{8,0},{1,9},{9,1},{2,10},{10,2},{3,11},{11,3},{4,12},{12,4},... | collective-permute-start | bytes 344072 | tf_op jit(solution)/shard_map/ppermute | solution.py:28
  54.7 2.2 %copy-start = (f32[128,5,1024]{2,0,1:T(8,128)}, f32[128,5,1024]{2,0,1:T(8,128)S(1)}, u32[]{:S(2)}) copy-start(f32[128,5,1024]{2,0,1:T(8,128)S(1)} %get-tuple-element.38) | copy-start | bytes 7864324
  61.1 3.4 %collective-permute-start.1 = (bf16[64,1,5,130]{3,0,2,1:T(8,128)(2,1)S(1)}, bf16[64,1,5,130]{3,0,2,1:T(8,128)(2,1)S(1)}, u32[]{:S(2)}, u32[]{:S(2)}) collective-permute-start(bf16[64,1,5,130]{3,0,2,1:T(8,128)(2,1)S(1)} %pad_maximum_fusion), channel_id=1, source_target_pairs={{0,8},{8,0},{1,9},{9,1},{2,10},{10,2},{3,11},{11,3},{4,12},{12,4},... | collective-permute-start | bytes 249608 | tf_op jit(solution)/shard_map/ppermute | solution.py:28
  96.0 8.5 %collective-permute-start.2 = (bf16[64,64,10]{0,1,2:T(8,128)(2,1)S(1)}, bf16[64,64,10]{0,1,2:T(8,128)(2,1)S(1)}, u32[]{:S(2)}, u32[]{:S(2)}) collective-permute-start(bf16[64,64,10]{0,1,2:T(8,128)(2,1)S(1)} %bitcast.304), channel_id=1, source_target_pairs={{0,1},{1,2},{2,3},{3,4},{4,5},{5,6},{6,7},{7,0},{8,9},{9,10},{10,1... | collective-permute-start | bytes 245768 | tf_op jit(solution)/shard_map/ppermute | solution.py:21
  104.6 8.4 %collective-permute-start.3 = (bf16[64,64,10]{0,1,2:T(8,128)(2,1)S(1)}, bf16[64,64,10]{0,1,2:T(8,128)(2,1)S(1)}, u32[]{:S(2)}, u32[]{:S(2)}) collective-permute-start(bf16[64,64,10]{0,1,2:T(8,128)(2,1)S(1)} %collective-permute-done.2), channel_id=1, source_target_pairs={{0,1},{1,2},{2,3},{3,4},{4,5},{5,6},{6,7},{7,0},{8,9},{9,10},{10,1... | collective-permute-start | bytes 245768 | tf_op jit(solution)/shard_map/ppermute | solution.py:21
  113.0 8.4 %collective-permute-start.4 = (bf16[64,64,10]{0,1,2:T(8,128)(2,1)S(1)}, bf16[64,64,10]{0,1,2:T(8,128)(2,1)S(1)}, u32[]{:S(2)}, u32[]{:S(2)}) collective-permute-start(bf16[64,64,10]{0,1,2:T(8,128)(2,1)S(1)} %collective-permute-done.3), channel_id=1, source_target_pairs={{0,1},{1,2},{2,3},{3,4},{4,5},{5,6},{6,7},{7,0},{8,9},{9,10},{10,1... | collective-permute-start | bytes 245768 | tf_op jit(solution)/shard_map/ppermute | solution.py:21
  121.4 8.4 %collective-permute-start.5 = (bf16[64,64,10]{0,1,2:T(8,128)(2,1)S(1)}, bf16[64,64,10]{0,1,2:T(8,128)(2,1)S(1)}, u32[]{:S(2)}, u32[]{:S(2)}) collective-permute-start(bf16[64,64,10]{0,1,2:T(8,128)(2,1)S(1)} %collective-permute-done.4), channel_id=1, source_target_pairs={{0,1},{1,2},{2,3},{3,4},{4,5},{5,6},{6,7},{7,0},{8,9},{9,10},{10,1... | collective-permute-start | bytes 245768 | tf_op jit(solution)/shard_map/ppermute | solution.py:21
  129.8 8.9 %collective-permute-start.6 = (bf16[64,64,10]{0,1,2:T(8,128)(2,1)S(1)}, bf16[64,64,10]{0,1,2:T(8,128)(2,1)S(1)}, u32[]{:S(2)}, u32[]{:S(2)}) collective-permute-start(bf16[64,64,10]{0,1,2:T(8,128)(2,1)S(1)} %collective-permute-done.5), channel_id=1, source_target_pairs={{0,1},{1,2},{2,3},{3,4},{4,5},{5,6},{6,7},{7,0},{8,9},{9,10},{10,1... | collective-permute-start | bytes 245768 | tf_op jit(solution)/shard_map/ppermute | solution.py:21
  138.7 10.0 %collective-permute-start.7 = (bf16[64,64,10]{0,1,2:T(8,128)(2,1)S(1)}, bf16[64,64,10]{0,1,2:T(8,128)(2,1)S(1)}, u32[]{:S(2)}, u32[]{:S(2)}) collective-permute-start(bf16[64,64,10]{0,1,2:T(8,128)(2,1)S(1)} %collective-permute-done.6), channel_id=1, source_target_pairs={{0,1},{1,2},{2,3},{3,4},{4,5},{5,6},{6,7},{7,0},{8,9},{9,10},{10,1... | collective-permute-start | bytes 245768 | tf_op jit(solution)/shard_map/ppermute | solution.py:21
  148.7 8.4 %collective-permute-start.8 = (bf16[64,64,10]{0,1,2:T(8,128)(2,1)S(1)}, bf16[64,64,10]{0,1,2:T(8,128)(2,1)S(1)}, u32[]{:S(2)}, u32[]{:S(2)}) collective-permute-start(bf16[64,64,10]{0,1,2:T(8,128)(2,1)S(1)} %collective-permute-done.7), channel_id=1, source_target_pairs={{0,1},{1,2},{2,3},{3,4},{4,5},{5,6},{6,7},{7,0},{8,9},{9,10},{10,1... | collective-permute-start | bytes 245768 | tf_op jit(solution)/shard_map/ppermute | solution.py:21
Sparse Core Ops, SparseCore 0:
  46.2 43.5 all-gather.1
